TPU v7x, 32 devices: a whole 2x2x4 slice. The times are simulated.
32 devices in a mesh: ctx: 16 (over z, y, x), tp: 2 (over core).
Axes of the slice: x: 2, y: 2, z: 4, core: 2. Of those that a mesh axis runs over, the one named last changes fastest.
Arguments:
- x_act: bfloat16 [4096, 8192], P('ctx', 'tp'), may hold values from -0.119628906 to 0.119628906
- b_proj: bfloat16 [4096, 128], P('ctx'), may hold values from -0.5 to 0.5
- c_proj: bfloat16 [4096, 128], P('ctx'), may hold values from -0.5 to 0.5
- dt_raw: bfloat16 [4096, 128], P('ctx', 'tp'), may hold values from -3 to 3
- a_log: float32 [128], P('tp'), may hold values from -12 to -2
- d_skip: float32 [128], P('tp'), may hold values from 0.5 to 2
- grad_out: bfloat16 [4096, 8192], P('ctx', 'tp'), may hold values from -6 to 6
Outputs:
- grad_x: bfloat16 [4096, 8192], P('ctx', 'tp')
- grad_b: float32 [4096, 128], P('ctx')
- grad_c: float32 [4096, 128], P('ctx')
- grad_dt: bfloat16 [4096, 128], P('ctx', 'tp')
All inputs are finite; a program needn't handle non-finite values.
Results may differ from a plain program's by a relative error of at most 0.001.
Values may be sent and summed in bfloat16 or wider, within the bound.
No kernel may reach another device: no remote copies, remote signals or barrier semaphores. Data moves between devices by JAX's collectives and lax.ppermute only.
A program may use at most 192 MiB of HBM per device.

v0:
```python
from functools import partial

import jax
import jax.numpy as jnp
from jax import lax
from jax.sharding import PartitionSpec as P

BLOCK = 256


precise = lax.Precision.HIGHEST


def head_forward(x_head, b_rows, c_rows, raw_step, log_rate, skip_gain, start_state, block_len):
    length, head_width = x_head.shape
    blocks = length // block_len
    step_size = jax.nn.softplus(raw_step)
    decay_rates = -jnp.exp(log_rate) * step_size
    row_index = lax.broadcasted_iota(jnp.int32, (block_len, block_len), 0)
    col_index = lax.broadcasted_iota(jnp.int32, (block_len, block_len), 1)
    lower_mask = row_index >= col_index
    running = jnp.dot(
        decay_rates.reshape(blocks, block_len), lower_mask.astype(jnp.float32).T, precision=precise
    )
    between = jnp.where(lower_mask[None], running[:, :, None] - running[:, None, :], -1e30)
    x_blocks = x_head.reshape(blocks, block_len, head_width)
    b_blocks = b_rows.reshape(blocks, block_len, -1)
    c_blocks = c_rows.reshape(blocks, block_len, -1)
    s_blocks = step_size.reshape(blocks, block_len)
    scores = (
        jnp.einsum("kin,kjn->kij", c_blocks, b_blocks, precision=precise)
        * jnp.exp(between)
        * s_blocks[:, None, :]
    )
    output = jnp.einsum("kij,kjp->kip", scores, x_blocks, precision=precise)
    closing = running[:, -1]
    weighted = (jnp.exp(closing[:, None] - running) * s_blocks)[:, :, None] * x_blocks
    states = jnp.einsum("kjp,kjn->kpn", weighted, b_blocks, precision=precise)
    block_rows = lax.broadcasted_iota(jnp.int32, (blocks, blocks), 0)
    block_cols = lax.broadcasted_iota(jnp.int32, (blocks, blocks), 1)
    through = jnp.dot((block_rows >= block_cols).astype(jnp.float32), closing, precision=precise)
    before = through - closing
    carry_weight = jnp.exp(
        jnp.where(block_rows > block_cols, before[:, None] - through[None, :], -1e30)
    )
    entering = (
        jnp.einsum("kj,jpn->kpn", carry_weight, states, precision=precise)
        + jnp.exp(before)[:, None, None] * start_state[None]
    )
    reading = jnp.exp(running)[:, :, None] * c_blocks
    output = output + jnp.einsum("kin,kpn->kip", reading, entering, precision=precise)
    output = output.reshape(length, head_width) + skip_gain * x_head
    final_state = (
        jnp.einsum("j,jpn->pn", jnp.exp(through[-1] - through), states, precision=precise)
        + jnp.exp(through[-1]) * start_state
    )
    return (output, final_state)


def local(x_act, b_proj, c_proj, dt_raw, a_log, d_skip, grad_out):
    heads_here = dt_raw.shape[1]
    head_width = x_act.shape[1] // heads_here
    runner = partial(head_forward, block_len=BLOCK)
    mapped = jax.vmap(runner, in_axes=(0, None, None, 0, 0, 0, 0))
    owners = lax.axis_size("ctx")
    per_owner = heads_here // owners
    x_seq, g_seq, raw_seq = (
        lax.all_to_all(x_act, "ctx", split_axis=1, concat_axis=0, tiled=True),
        lax.all_to_all(grad_out, "ctx", split_axis=1, concat_axis=0, tiled=True),
        lax.all_to_all(dt_raw, "ctx", split_axis=1, concat_axis=0, tiled=True),
    )
    b_seq, c_seq = (
        lax.all_gather(b_proj, "ctx", axis=0, tiled=True),
        lax.all_gather(c_proj, "ctx", axis=0, tiled=True),
    )
    first_head = lax.axis_index("ctx") * per_owner
    rate_own = lax.dynamic_slice_in_dim(a_log, first_head, per_owner)
    gain_own = lax.dynamic_slice_in_dim(d_skip, first_head, per_owner)
    length = x_seq.shape[0]
    x_heads = x_seq.astype(jnp.float32).reshape(length, per_owner, head_width).transpose(1, 0, 2)
    g_heads = g_seq.astype(jnp.float32).reshape(length, per_owner, head_width).transpose(1, 0, 2)
    raw_heads = raw_seq.astype(jnp.float32).T
    b_rows = b_seq.astype(jnp.float32)
    c_rows = c_seq.astype(jnp.float32)
    anchor = jnp.zeros((per_owner, head_width, b_rows.shape[1]), jnp.float32)

    def forward(x_val, b_val, c_val, raw_val):
        return mapped(x_val, b_val, c_val, raw_val, rate_own, gain_own, anchor)[0]

    outcome, pullback = jax.vjp(forward, x_heads, b_rows, c_rows, raw_heads)
    grad_xh, grad_b_all, grad_c_all, grad_raw = pullback(g_heads)
    x_back = grad_xh.transpose(1, 0, 2).reshape(length, per_owner * head_width).astype(jnp.bfloat16)
    raw_back = grad_raw.T.astype(jnp.bfloat16)
    grad_x, grad_dt = (
        lax.all_to_all(x_back, "ctx", split_axis=0, concat_axis=1, tiled=True),
        lax.all_to_all(raw_back, "ctx", split_axis=0, concat_axis=1, tiled=True),
    )
    part_b, part_c = (
        lax.psum_scatter(grad_b_all, "ctx", scatter_dimension=0, tiled=True),
        lax.psum_scatter(grad_c_all, "ctx", scatter_dimension=0, tiled=True),
    )
    grad_b, grad_c = lax.psum((part_b, part_c), "tp")
    return (grad_x, grad_b, grad_c, grad_dt)


def solution(mesh):
    in_specs = (
        P("ctx", "tp"),
        P("ctx", None),
        P("ctx", None),
        P("ctx", "tp"),
        P("tp"),
        P("tp"),
        P("ctx", "tp"),
    )
    out_specs = (P("ctx", "tp"), P("ctx", None), P("ctx", None), P("ctx", "tp"))
    return jax.shard_map(local, mesh=mesh, in_specs=in_specs, out_specs=out_specs, check_vma=False)
```

profile of v0, /device:TPU:12, one launch (start us, length us, event | category | flops | bytes accessed | tf_op | source)
XLA Modules:
  0.0 437.3 jit_solution(15441246282450113212)
XLA Ops:
  8.6 7.2 %all-to-all-start.1 = ((bf16[256,16,4]{0,2,1:T(4,128)(2,1)}), bf16[256,16,4]{0,2,1:T(4,128)(2,1)S(1)}, u32[]{:S(2)}, u32[]{:S(2)}) async-start(bf16[256,16,4]{0,2,1:T(4,128)(2,1)} %all_to_all.68), calls=%async_computation.1 | async-start | bytes 65536 | tf_op jit(solution)/shard_map/all_to_all | solution.py:70
  15.7 4.1 copy.86
  20.9 5.8 %all-to-all-start.3 = ((bf16[256,16,256]{0,2,1:T(8,128)(2,1)}), bf16[256,16,256]{0,2,1:T(8,128)(2,1)S(1)}, u32[]{:S(2)}, u32[]{:S(2)}) async-start(bf16[256,16,256]{0,2,1:T(8,128)(2,1)} %bitcast.188), calls=%async_computation.3 | async-start | bytes 4194304 | tf_op jit(solution)/shard_map/all_to_all | solution.py:68
  27.5 4.2 copy.73
  31.6 47.1 %all-to-all-done.3 = bf16[256,16,256]{0,2,1:T(8,128)(2,1)S(1)} async-done(((bf16[256,16,256]{0,2,1:T(8,128)(2,1)}), bf16[256,16,256]{0,2,1:T(8,128)(2,1)S(1)}, u32[]{:S(2)}, u32[]{:S(2)}) %all-to-all-start.3) | async-done | bytes 2097184 | tf_op jit(solution)/shard_map/all_to_all | solution.py:68
  78.7 4.8 %all-to-all-start = ((bf16[256,16,256]{0,2,1:T(8,128)(2,1)}), bf16[256,16,256]{0,2,1:T(8,128)(2,1)}, u32[]{:S(2)}, u32[]{:S(2)}) async-start(bf16[256,16,256]{0,2,1:T(8,128)(2,1)} %bitcast.186), calls=%async_computation | async-start | bytes 4194304 | tf_op jit(solution)/shard_map/all_to_all | solution.py:69
  86.4 18.9 %all-gather.3.cloned.1.call-done = bf16[4096,128]{1,0:T(8,128)(2,1)} async-done(((bf16[256,128]{1,0:T(8,128)(2,1)}), bf16[4096,128]{1,0:T(8,128)(2,1)}) %all-gather.3.cloned.1.call-update) | async-done | bytes 1048592 | tf_op jit(solution)/shard_map/all_gather | solution.py:74
  108.0 65.0 %all-gather.5.cloned.1.call-done = bf16[4096,128]{1,0:T(8,128)(2,1)} async-done(((bf16[256,128]{1,0:T(8,128)(2,1)}), bf16[4096,128]{1,0:T(8,128)(2,1)}) %all-gather.5.cloned.1.call-update) | async-done | bytes 1048592 | tf_op jit(solution)/shard_map/all_gather | solution.py:73
  182.3 4.1 copy.74
  186.4 4.4 %all_to_all.67 = bf16[4096,4,64]{0,2,1:T(8,128)(2,1)} reshape(bf16[16,256,256]{1,0,2:T(8,128)(2,1)} %copy.74) | data formatting | bytes 4194304 | tf_op jit(solution)/shard_map/all_to_all | solution.py:69
  190.8 8.1 %multiply_reduce_fusion.2 = (f32[4,16]{1,0:T(4,128)}, f32[4,16,64,128]{3,2,1,0:T(8,128)S(1)}) fusion(bf16[4,8,16,8,256]{4,3,2,1,0:T(8,128)(2,1)} %bitcast.173, f32[16,256,128]{1,2,0:T(8,128)} %copy.76, f32[4,16,256]{2,1,0:T(8,128)S(1)} %get-tuple-element.30), kind=kOutput, calls=%fused_computation.41 | convolution fusion | flops 1613758464 | bytes 6357248 | tf_op jit(solution)/shard_map/transpose(jvp(vmap(kin,kpn->kip)))/dot_general | solution.py:51
  202.1 4.5 %fusion.12 = (f32[4,16,256]{2,0,1:T(4,128)S(1)}, f32[16,4,64,256]{3,2,1,0:T(8,128)}) fusion(bf16[4,8,16,8,256]{4,3,2,1,0:T(8,128)(2,1)S(1)} %bitcast.169, bf16[16,256,128,1]{2,1,3,0:T(8,128)(2,1)S(1)} %bitcast.179, f32[16,4,64,128]{3,0,2,1:T(8,128)S(1)} %fusion.46), kind=kOutput, calls=%fused_computation.20 | convolution fusion | flops 1613742080 | bytes 9502720 | tf_op jit(solution)/shard_map/transpose(jvp(vmap(kjp,kjn->kpn)))/dot_general | solution.py:38
  206.7 15.7 %fusion.5 = (f32[4,16,256]{2,1,0:T(8,128)}, f32[4,16,256]{2,1,0:T(8,128)}, f32[4,16,256]{2,1,0:T(8,128)S(1)}, f32[16,256,256]{2,1,0:T(8,128)S(1)}, f32[4,16,256,256]{3,2,1,0:T(8,128)}) fusion(f32[4,16,256]{2,1,0:T(8,128)S(1)} %bitcast.202, f32[4,16,256]{2,1,0:T(8,128)S(1)} %get-tuple-element.31, f32[16,256,256]{2,1,0:T(8,128)S(1)} %copy-done.9, ...), kind=kOutput, calls=%fused_computation.9 | convolution fusion | flops 594493440 | bytes 29753344 | tf_op jit(solution)/shard_map/transpose(jvp(vmap(kij,kjp->kip)))/dot_general | solution.py:35
  227.7 8.7 %bitcast_add_fusion.1 = f32[16,256,128]{2,1,0:T(8,128)} fusion(f32[16,256,128]{2,1,0:T(8,128)S(1)} %fusion.123, f32[16,4,64,128]{3,0,2,1:T(8,128)S(1)} %fusion.46, f32[4,16,256]{2,0,1:T(4,128)S(1)} %copy.75, bf16[4,8,16,8,256]{4,3,2,1,0:T(8,128)(2,1)S(1)} %bitcast.171), kind=kOutput, calls=%fused_computation.39 | convolution fusion | flops 1613234176 | bytes 8454144 | tf_op jit(solution)/shard_map/transpose(jvp(vmap(kjp,kjn->kpn)))/dot_general | solution.py:38
  237.7 11.3 %fusion.14 = f32[16,4,8,8,256]{4,3,2,1,0:T(8,128)S(1)} fusion(f32[16,4,64,256]{3,2,1,0:T(8,128)} %get-tuple-element.34, f32[4,16,256]{2,0,1:T(4,128)S(1)} %copy.75, bf16[4,8,16,8,256]{4,3,2,1,0:T(8,128)(2,1)} %bitcast.174, f32[4,16,256,256]{3,2,1,0:T(8,128)} %get-tuple-element.24), kind=kOutput, calls=%fused_computation.23 | convolution fusion | flops 3223322624 | bytes 27328512 | tf_op jit(solution)/shard_map/transpose(jvp(vmap(kij,kjp->kip)))/dot_general | solution.py:35
  254.0 5.3 %fusion.120 = (f32[4,16]{1,0:T(4,128)S(1)}, f32[4,16]{1,0:T(4,128)S(1)}) fusion(f32[4,16]{1,0:T(4,128)S(1)} %get-tuple-element.32, f32[4,16]{1,0:T(4,128)S(1)} %get-tuple-element.23, f32[16,4,64,128]{3,2,1,0:T(8,128)S(1)} %fusion.10, f32[4,16,64,128]{3,2,1,0:T(8,128)S(1)} %copy-done.8, pred[16,16]{1,0:T(8,128)(4,1)S(1)} %iota_compare_fusion.6), kind=kOutput, calls=%fused_computation.124 | convolution fusion | flops 100669312 | bytes 4195584 | tf_op jit(solution)/shard_map/transpose(jvp(vmap(kj,jpn->kpn)))/dot_general | solution.py:47
  260.1 4.6 %fusion.49 = f32[4,16,64,128]{3,1,2,0:T(8,128)S(1)} fusion(f32[16,4,64,128]{3,2,1,0:T(8,128)} %copy-done, f32[4,16]{1,0:T(4,128)} %get-tuple-element.22, f32[4,16]{1,0:T(4,128)S(1)} %get-tuple-element.32, f32[4,16]{1,0:T(4,128)S(1)} %get-tuple-element.23, pred[16,16]{1,0:T(8,128)(4,1)S(1)} %iota_compare_fusion.6), kind=kOutput, calls=%fused_computation.55 | convolution fusion | flops 101189632 | bytes 4195328 | tf_op jit(solution)/shard_map/jvp(vmap(kj,jpn->kpn))/dot_general | solution.py:47
  264.8 7.2 %fusion.7 = (f32[4,16,256]{2,1,0:T(8,128)S(1)}, f32[16,256,128]{1,2,0:T(8,128)}) fusion(f32[16,256,128]{1,2,0:T(8,128)S(1)} %copy-done.10, f32[4,16,256]{2,1,0:T(8,128)S(1)} %copy-done.14, bf16[4,8,16,8,256]{4,3,2,1,0:T(8,128)(2,1)S(1)} %bitcast.176, f32[4,16,64,128]{3,1,2,0:T(8,128)S(1)} %fusion.49), kind=kOutput, calls=%fused_computation.13 | convolution fusion | flops 1618460672 | bytes 8519680 | tf_op jit(solution)/shard_map/transpose(jvp(vmap(kin,kpn->kip)))/dot_general | solution.py:51
  273.0 5.9 %all-to-all-start.4 = ((bf16[16,256,4]{1,2,0:T(4,128)(2,1)}), bf16[16,256,4]{1,2,0:T(4,128)(2,1)S(1)}, u32[]{:S(2)}, u32[]{:S(2)}) async-start(bf16[16,256,4]{1,2,0:T(4,128)(2,1)} %bitcast.37), calls=%async_computation.6 | async-start | bytes 65536 | tf_op jit(solution)/shard_map/all_to_all | solution.py:96
  281.9 6.3 %convolution_add_fusion = f32[16,256,128]{2,1,0:T(8,128)} fusion(f32[16,256,128]{2,1,0:T(8,128)} %copy.96, f32[16,256,256]{2,1,0:T(8,128)} %copy-done.3, bf16[16,256,128]{2,1,0:T(8,128)(2,1)S(1)} %bitcast.181), kind=kOutput, calls=%fused_computation.57 | convolution fusion | flops 1611137024 | bytes 9437184 | tf_op jit(solution)/shard_map/transpose(jvp(vmap(kin,kjn->kij)))/dot_general | solution.py:31
  294.4 6.9 %all-to-all-start.2 = ((bf16[16,256,256]{1,2,0:T(8,128)(2,1)}), bf16[16,256,256]{1,2,0:T(8,128)(2,1)S(1)}, u32[]{:S(2)}, u32[]{:S(2)}) async-start(bf16[16,256,256]{1,2,0:T(8,128)(2,1)} %copy.85), calls=%async_computation.2 | async-start | bytes 4194304 | tf_op jit(solution)/shard_map/all_to_all | solution.py:95
  301.3 8.9 %reduce-scatter.3.cloned.1.call-done = f32[256,128]{1,0:T(8,128)} async-done(((f32[4096,128]{1,0:T(8,128)}), f32[256,128]{1,0:T(8,128)}) %reduce-scatter.3.cloned.1.call-update) | async-done | bytes 131088 | tf_op jit(solution)/shard_map/reduce_scatter | solution.py:99
  310.3 90.6 %reduce-scatter.5.cloned.1.call-done = f32[256,128]{1,0:T(8,128)} async-done(((f32[4096,128]{1,0:T(8,128)}), f32[256,128]{1,0:T(8,128)}) %reduce-scatter.5.cloned.1.call-update) | async-done | bytes 131088 | tf_op jit(solution)/shard_map/reduce_scatter | solution.py:100
  404.4 23.1 %all-reduce.4.cloned.1.call-done = (f32[256,128]{1,0:T(8,128)}, f32[256,128]{1,0:T(8,128)}) async-done(((f32[256,128]{1,0:T(8,128)}, f32[256,128]{1,0:T(8,128)}), (f32[256,128]{1,0:T(8,128)}, f32[256,128]{1,0:T(8,128)})) %all-reduce.4.cloned.1.call-update) | async-done | bytes 262160 | tf_op jit(solution)/shard_map/psum | solution.py:102
  (99 shorter events, 50.5 us)
Async XLA Ops:
  8.6 12.4 %all-to-all-start.1 = ((bf16[256,16,4]{0,2,1:T(4,128)(2,1)}), bf16[256,16,4]{0,2,1:T(4,128)(2,1)S(1)}, u32[]{:S(2)}, u32[]{:S(2)}) async-start(bf16[256,16,4]{0,2,1:T(4,128)(2,1)} %all_to_all.68), calls=%async_computation.1 | async-start | bytes 65536 | tf_op jit(solution)/shard_map/all_to_all | solution.py:70
  20.9 57.8 %all-to-all-start.3 = ((bf16[256,16,256]{0,2,1:T(8,128)(2,1)}), bf16[256,16,256]{0,2,1:T(8,128)(2,1)S(1)}, u32[]{:S(2)}, u32[]{:S(2)}) async-start(bf16[256,16,256]{0,2,1:T(8,128)(2,1)} %bitcast.188), calls=%async_computation.3 | async-start | bytes 4194304 | tf_op jit(solution)/shard_map/all_to_all | solution.py:68
  26.8 78.5 %all-gather.3.cloned.1.call-start = ((), (), s32[]{:S(2)}) async-start(), calls=%async_computation.7 | async-start | bytes 1114112 | tf_op jit(solution)/shard_map/all_gather | solution.py:74
  78.7 5.6 %copy-start.22 = (f32[64]{0:T(128)S(1)}, f32[64]{0:T(128)}, u32[]{:S(2)}) copy-start(f32[64]{0:T(128)} %param.11) | copy-start | bytes 772
  78.7 103.5 %all-to-all-start = ((bf16[256,16,256]{0,2,1:T(8,128)(2,1)}), bf16[256,16,256]{0,2,1:T(8,128)(2,1)}, u32[]{:S(2)}, u32[]{:S(2)}) async-start(bf16[256,16,256]{0,2,1:T(8,128)(2,1)} %bitcast.186), calls=%async_computation | async-start | bytes 4194304 | tf_op jit(solution)/shard_map/all_to_all | solution.py:69
  83.5 89.5 %all-gather.5.cloned.1.call-start = ((), (), s32[]{:S(2)}) async-start(), calls=%async_computation.8 | async-start | bytes 1114112 | tf_op jit(solution)/shard_map/all_gather | solution.py:73
  84.3 226.0 %reduce-scatter.3.cloned.1.call-start = ((), (), s32[]{:S(2)}) async-start(), calls=%async_computation.9 | async-start | bytes 2228224 | tf_op jit(solution)/shard_map/reduce_scatter | solution.py:99
  85.5 105.2 %copy-start.13 = (f32[4,16,256]{2,1,0:T(8,128)}, f32[4,16,256]{2,1,0:T(8,128)S(1)}, u32[]{:S(2)}) copy-start(f32[4,16,256]{2,1,0:T(8,128)S(1)} %get-tuple-element.30) | copy-start | bytes 196612
  105.3 67.7 %copy-start.5 = (bf16[4096,128]{1,0:T(8,128)(2,1)S(1)}, bf16[4096,128]{1,0:T(8,128)(2,1)}, u32[]{:S(2)}) copy-start(bf16[4096,128]{1,0:T(8,128)(2,1)} %all-gather.3.cloned.1.call-done) | copy-start | bytes 3145732
  206.7 17.5 %copy-start.6 = (bf16[4096,128]{1,0:T(8,128)(2,1)S(1)}, bf16[4096,128]{1,0:T(8,128)(2,1)}, u32[]{:S(2)}) copy-start(bf16[4096,128]{1,0:T(8,128)(2,1)} %all-gather.3.cloned.1.call-done) | copy-start | bytes 3145732
  222.4 5.3 %copy-start.3 = (f32[16,256,256]{2,1,0:T(8,128)}, f32[16,256,256]{2,1,0:T(8,128)S(1)}, u32[]{:S(2)}) copy-start(f32[16,256,256]{2,1,0:T(8,128)S(1)} %get-tuple-element.15) | copy-start | bytes 12582916
  253.9 5.3 %copy-start = (f32[16,4,64,128]{3,2,1,0:T(8,128)}, f32[16,4,64,128]{3,2,1,0:T(8,128)S(1)}, u32[]{:S(2)}) copy-start(f32[16,4,64,128]{3,2,1,0:T(8,128)S(1)} %fusion.10) | copy-start | bytes 6291460
  253.9 5.3 %copy-start.18 = (f32[4,16]{1,0:T(4,128)S(1)}, f32[4,16]{1,0:T(4,128)}, u32[]{:S(2)}) copy-start(f32[4,16]{1,0:T(4,128)} %get-tuple-element.25) | copy-start | bytes 772
  254.0 5.3 %copy-start.24 = (f32[4,16]{1,0:T(4,128)S(1)}, f32[4,16]{1,0:T(4,128)}, u32[]{:S(2)}) copy-start(f32[4,16]{1,0:T(4,128)} %get-tuple-element.35) | copy-start | bytes 772
  254.0 10.7 %copy-start.14 = (f32[4,16,256]{2,1,0:T(8,128)S(1)}, f32[4,16,256]{2,1,0:T(8,128)}, u32[]{:S(2)}) copy-start(f32[4,16,256]{2,1,0:T(8,128)} %copy-done.13) | copy-start | bytes 196612
  260.1 4.6 %copy-start.10 = (f32[16,256,128]{1,2,0:T(8,128)S(1)}, f32[16,256,128]{1,2,0:T(8,128)}, u32[]{:S(2)}) copy-start(f32[16,256,128]{1,2,0:T(8,128)} %copy.76) | copy-start | bytes 6291460
  264.7 7.2 %copy-start.12 = (f32[4,16,1]{2,1,0:T(8,128)S(1)}, f32[4,16,1]{2,1,0:T(8,128)}, u32[]{:S(2)}) copy-start(f32[4,16,1]{2,1,0:T(8,128)} %copy.101) | copy-start | bytes 772
  264.7 7.2 %copy-start.15 = (f32[4,16,256]{2,1,0:T(8,128)S(1)}, f32[4,16,256]{2,1,0:T(8,128)}, u32[]{:S(2)}) copy-start(f32[4,16,256]{2,1,0:T(8,128)} %get-tuple-element.12) | copy-start | bytes 196612
  264.8 7.2 %copy-start.16 = (f32[4,16,256]{2,1,0:T(8,128)S(1)}, f32[4,16,256]{2,1,0:T(8,128)}, u32[]{:S(2)}) copy-start(f32[4,16,256]{2,1,0:T(8,128)} %get-tuple-element.13) | copy-start | bytes 196612
  264.8 7.5 %copy-start.20 = (f32[4]{0:T(128)S(1)}, f32[4]{0:T(128)}, u32[]{:S(2)}) copy-start(f32[4]{0:T(128)} %copy-done.19) | copy-start | bytes 52
  273.0 21.3 %all-to-all-start.4 = ((bf16[16,256,4]{1,2,0:T(4,128)(2,1)}), bf16[16,256,4]{1,2,0:T(4,128)(2,1)S(1)}, u32[]{:S(2)}, u32[]{:S(2)}) async-start(bf16[16,256,4]{1,2,0:T(4,128)(2,1)} %bitcast.37), calls=%async_computation.6 | async-start | bytes 65536 | tf_op jit(solution)/shard_map/all_to_all | solution.py:96
  278.9 122.0 %reduce-scatter.5.cloned.1.call-start = ((), (), s32[]{:S(2)}) async-start(), calls=%async_computation.10 | async-start | bytes 2228224 | tf_op jit(solution)/shard_map/reduce_scatter | solution.py:100
  294.4 107.1 %all-to-all-start.2 = ((bf16[16,256,256]{1,2,0:T(8,128)(2,1)}), bf16[16,256,256]{1,2,0:T(8,128)(2,1)S(1)}, u32[]{:S(2)}, u32[]{:S(2)}) async-start(bf16[16,256,256]{1,2,0:T(8,128)(2,1)} %copy.85), calls=%async_computation.2 | async-start | bytes 4194304 | tf_op jit(solution)/shard_map/all_to_all | solution.py:95
  301.3 126.2 %all-reduce.4.cloned.1.call-start = ((), (), s32[]{:S(2)}) async-start(), calls=%async_computation.11 | async-start | bytes 524288 | tf_op jit(solution)/shard_map/psum | solution.py:102
  (11 other events, 31.7 us)
Sparse Core Ops, SparseCore 0:
  30.3 74.9 all-gather.2
  108.0 64.9 all-gather.4
  236.6 73.6 reduce-scatter.2
  312.4 88.4 reduce-scatter.4
  403.1 24.3 all-reduce.3
where the time goes:
time: 444 us; the launch traced here: 437 us
  waiting for transfers between devices  256 us (58%)
  matrix products  85.8 us (19%)
  local copies, waits for them, and re-layouts  44.6 us (10%)
  starting transfers between devices  30.7 us (7%)
  between operations  14.4 us (3%)
  other arithmetic  5.62 us (1%)
    reduce_scatter x1, waiting for transfers between devices, local(): lax.psum_scatter(grad_c_all, 'ctx', scatter_dimension=0, tiled=True)  90.6 us
    all_gather x1, waiting for transfers between devices, local(): lax.all_gather(b_proj, 'ctx', axis=0, tiled=True)  65 us
    all_to_all x1, waiting for transfers between devices, local(): lax.all_to_all(x_act, 'ctx', split_axis=1, concat_axis=0, tiled=True)  47.1 us
    dot_general x2, matrix products, head_forward(): output = jnp.einsum('kij,kjp->kip', scores, x_blocks, precision=precise)  26.9 us
    psum x1, waiting for transfers between devices, local(): grad_b, grad_c = lax.psum((part_b, part_c), 'tp')  23.1 us
    all_gather x1, waiting for transfers between devices, local(): lax.all_gather(c_proj, 'ctx', axis=0, tiled=True)  18.9 us
    unnamed x59, local copies, waits for them, and re-layouts  17 us
    dot_general x3, matrix products, head_forward(): states = jnp.einsum('kjp,kjn->kpn', weighted, b_blocks, precision=precise)  15.5 us
  transfers between devices with their start and end apart: 10, of which 7 were waited for; matrix products, arithmetic and copies ran while one was open for 17% of the time, Pallas kernels for 0%

commit v1 on v0

--- a/solution.py
+++ b/solution.py
@@ -57,49 +57,88 @@
     return (output, final_state)
 
 
+N_CHUNKS = 1
+
+
+def chunk_backward(x_seq, g_seq, raw_seq, b_rows, c_rows, rate, gain):
+    length = x_seq.shape[0]
+    heads = raw_seq.shape[1]
+    head_width = x_seq.shape[1] // heads
+    runner = partial(head_forward, block_len=BLOCK)
+    mapped = jax.vmap(runner, in_axes=(0, None, None, 0, 0, 0, 0))
+    x_heads = x_seq.astype(jnp.float32).reshape(length, heads, head_width).transpose(1, 0, 2)
+    g_heads = g_seq.astype(jnp.float32).reshape(length, heads, head_width).transpose(1, 0, 2)
+    raw_heads = raw_seq.astype(jnp.float32).T
+    anchor = jnp.zeros((heads, head_width, b_rows.shape[1]), jnp.float32)
+
+    def forward(x_val, b_val, c_val, raw_val):
+        return mapped(x_val, b_val, c_val, raw_val, rate, gain, anchor)[0]
+
+    _, pullback = jax.vjp(forward, x_heads, b_rows, c_rows, raw_heads)
+    grad_xh, grad_b_all, grad_c_all, grad_raw = pullback(g_heads)
+    x_back = grad_xh.transpose(1, 0, 2).reshape(length, heads * head_width).astype(jnp.bfloat16)
+    raw_back = grad_raw.T.astype(jnp.bfloat16)
+    return x_back, raw_back, grad_b_all, grad_c_all
+
+
 def local(x_act, b_proj, c_proj, dt_raw, a_log, d_skip, grad_out):
+    rows = x_act.shape[0]
     heads_here = dt_raw.shape[1]
     head_width = x_act.shape[1] // heads_here
-    runner = partial(head_forward, block_len=BLOCK)
-    mapped = jax.vmap(runner, in_axes=(0, None, None, 0, 0, 0, 0))
+    state = b_proj.shape[1]
     owners = lax.axis_size("ctx")
     per_owner = heads_here // owners
-    x_seq, g_seq, raw_seq = (
-        lax.all_to_all(x_act, "ctx", split_axis=1, concat_axis=0, tiled=True),
-        lax.all_to_all(grad_out, "ctx", split_axis=1, concat_axis=0, tiled=True),
-        lax.all_to_all(dt_raw, "ctx", split_axis=1, concat_axis=0, tiled=True),
-    )
-    b_seq, c_seq = (
-        lax.all_gather(b_proj, "ctx", axis=0, tiled=True),
-        lax.all_gather(c_proj, "ctx", axis=0, tiled=True),
-    )
-    first_head = lax.axis_index("ctx") * per_owner
+    chunks = N_CHUNKS if per_owner % N_CHUNKS == 0 else 1
+    per_chunk = per_owner // chunks
+    me = lax.axis_index("ctx")
+    half = lax.axis_index("tp")
+
+    bc_seq = lax.all_gather(jnp.concatenate([b_proj, c_proj], axis=1), "ctx", axis=0, tiled=True)
+    b_rows = bc_seq[:, :state].astype(jnp.float32)
+    c_rows = bc_seq[:, state:].astype(jnp.float32)
+    first_head = me * per_owner
     rate_own = lax.dynamic_slice_in_dim(a_log, first_head, per_owner)
     gain_own = lax.dynamic_slice_in_dim(d_skip, first_head, per_owner)
-    length = x_seq.shape[0]
-    x_heads = x_seq.astype(jnp.float32).reshape(length, per_owner, head_width).transpose(1, 0, 2)
-    g_heads = g_seq.astype(jnp.float32).reshape(length, per_owner, head_width).transpose(1, 0, 2)
-    raw_heads = raw_seq.astype(jnp.float32).T
-    b_rows = b_seq.astype(jnp.float32)
-    c_rows = c_seq.astype(jnp.float32)
-    anchor = jnp.zeros((per_owner, head_width, b_rows.shape[1]), jnp.float32)
 
-    def forward(x_val, b_val, c_val, raw_val):
-        return mapped(x_val, b_val, c_val, raw_val, rate_own, gain_own, anchor)[0]
+    x4 = x_act.reshape(rows, owners, per_owner, head_width)
+    g4 = grad_out.reshape(rows, owners, per_owner, head_width)
+    r3 = dt_raw.reshape(rows, owners, per_owner)
+    x_parts, raw_parts = [], []
+    grad_b_all = None
+    grad_c_all = None
+    for c in range(chunks):
+        sl = slice(c * per_chunk, (c + 1) * per_chunk)
+        width = per_chunk * head_width
+        xg = jnp.concatenate(
+            [x4[:, :, sl, :].reshape(rows, owners, width), g4[:, :, sl, :].reshape(rows, owners, width)], axis=2
+        )
+        xg_seq = lax.all_to_all(xg, "ctx", split_axis=1, concat_axis=0, tiled=True).reshape(rows * owners, 2 * width)
+        raw_seq = lax.all_to_all(r3[:, :, sl], "ctx", split_axis=1, concat_axis=0, tiled=True).reshape(
+            rows * owners, per_chunk
+        )
+        x_back, raw_back, gb, gc = chunk_backward(
+            xg_seq[:, :width], xg_seq[:, width:], raw_seq, b_rows, c_rows, rate_own[sl], gain_own[sl]
+        )
+        x_parts.append(
+            lax.all_to_all(x_back, "ctx", split_axis=0, concat_axis=1, tiled=True).reshape(rows, owners, 1, width)
+        )
+        raw_parts.append(
+            lax.all_to_all(raw_back, "ctx", split_axis=0, concat_axis=1, tiled=True).reshape(rows, owners, 1, per_chunk)
+        )
+        grad_b_all = gb if grad_b_all is None else grad_b_all + gb
+        grad_c_all = gc if grad_c_all is None else grad_c_all + gc
+    grad_x = jnp.concatenate(x_parts, axis=2).reshape(rows, owners * per_owner * head_width)
+    grad_dt = jnp.concatenate(raw_parts, axis=2).reshape(rows, heads_here)
 
-    outcome, pullback = jax.vjp(forward, x_heads, b_rows, c_rows, raw_heads)
-    grad_xh, grad_b_all, grad_c_all, grad_raw = pullback(g_heads)
-    x_back = grad_xh.transpose(1, 0, 2).reshape(length, per_owner * head_width).astype(jnp.bfloat16)
-    raw_back = grad_raw.T.astype(jnp.bfloat16)
-    grad_x, grad_dt = (
-        lax.all_to_all(x_back, "ctx", split_axis=0, concat_axis=1, tiled=True),
-        lax.all_to_all(raw_back, "ctx", split_axis=0, concat_axis=1, tiled=True),
-    )
-    part_b, part_c = (
-        lax.psum_scatter(grad_b_all, "ctx", scatter_dimension=0, tiled=True),
-        lax.psum_scatter(grad_c_all, "ctx", scatter_dimension=0, tiled=True),
-    )
-    grad_b, grad_c = lax.psum((part_b, part_c), "tp")
+    is_first = half == 0
+    send = jnp.where(is_first, grad_c_all, grad_b_all)
+    keep = jnp.where(is_first, grad_b_all, grad_c_all)
+    mine = keep + lax.ppermute(send, "tp", [(0, 1), (1, 0)])
+    parts = lax.all_to_all(mine.reshape(owners, rows, state), "ctx", split_axis=0, concat_axis=0, tiled=True)
+    mine = parts.sum(axis=0)
+    other = lax.ppermute(mine, "tp", [(0, 1), (1, 0)])
+    grad_b = jnp.where(is_first, mine, other)
+    grad_c = jnp.where(is_first, other, mine)
     return (grad_x, grad_b, grad_c, grad_dt)
 
 

time: 444 us -> 373 us (0.84)
  waiting for transfers between devices: 256 us -> 185 us
  other arithmetic: 5.62 us -> 12.7 us
    reduce_scatter x2 -> x0, waiting for transfers between devices: 99.5 us -> none  [the longest x1 90.6 us: local(): lax.psum_scatter(grad_c_all, 'ctx', scatter_dimension=0, tiled=True)]
    all_to_all x1, waiting for transfers between devices: 0.01 us -> 45.2 us  [local(): lax.all_to_all(x_back, 'ctx', split_axis=0, concat_axis=1, tiled=True)]
    psum x1 -> x0, waiting for transfers between devices: 23.1 us -> none  [local(): grad_b, grad_c = lax.psum((part_b, part_c), 'tp')]
    all_gather x2 -> x1, waiting for transfers between devices: 83.9 us -> 104 us  [local(): lax.all_gather(jnp.concatenate([b_proj, c_proj], axis=1), 'ctx', axis=0,...]
    all_to_all x3, waiting for transfers between devices: 48.2 us -> 33.2 us  [the longest x1 33.2 us: local(): lax.all_to_all(mine.reshape(owners, rows, state), 'ctx', split_axis=0, co...]
    slice x0 -> x4, local copies, waits for them, and re-layouts: none -> 13.4 us  [the longest x2 7.43 us: local(): xg_seq[:, :width]]
    all_to_all x5 -> x1, local copies, waits for them, and re-layouts: 15.2 us -> 6.46 us  [local(): lax.all_to_all(xg, 'ctx', split_axis=1, concat_axis=0, tiled=True)]
    concatenate x0 -> x2, other arithmetic: none -> 4.57 us  [the longest x1 3.9 us: local(): jnp.concatenate([x4[:, :, sl, :].reshape(rows, owners, width), g4[:, :, s...]
  transfers between devices with their start and end apart: 10 -> 8, of which waited for: 7 -> 4; matrix products, arithmetic and copies ran while one was open for 17% -> 13% of each run, Pallas kernels for 0% -> 0%
where the time goes in v1:
time: 373 us; the launch traced here: 369 us
  waiting for transfers between devices  185 us (50%)
  matrix products  82.4 us (22%)
  local copies, waits for them, and re-layouts  42.3 us (11%)
  starting transfers between devices  31.3 us (8%)
  between operations  14.7 us (4%)
  other arithmetic  12.7 us (3%)
    all_gather x1, waiting for transfers between devices, local(): lax.all_gather(jnp.concatenate([b_proj, c_proj], axis=1), 'ctx', axis=0,...  104 us
    all_to_all x1, waiting for transfers between devices, local(): lax.all_to_all(x_back, 'ctx', split_axis=0, concat_axis=1, tiled=True)  45.2 us
    all_to_all x1, waiting for transfers between devices, local(): lax.all_to_all(mine.reshape(owners, rows, state), 'ctx', split_axis=0, co...  33.2 us
    dot_general x2, matrix products, head_forward(): output = jnp.einsum('kij,kjp->kip', scores, x_blocks, precision=precise)  26 us
    dot_general x3, matrix products, head_forward(): states = jnp.einsum('kjp,kjn->kpn', weighted, b_blocks, precision=precise)  15.8 us
    dot_general x2, matrix products, head_forward(): jnp.einsum('kin,kpn->kip', reading, entering, precision=precise)  15.2 us
    unnamed x67, local copies, waits for them, and re-layouts  13 us
    dot_general x3, matrix products, head_forward(): jnp.einsum('kin,kjn->kij', c_blocks, b_blocks, precision=precise)  12.8 us
  transfers between devices with their start and end apart: 8, of which 4 were waited for; matrix products, arithmetic and copies ran while one was open for 13% of the time, Pallas kernels for 0%

profile of v1, /device:TPU:12, one launch (start us, length us, event | category | flops | bytes accessed | tf_op | source)
XLA Modules:
  0.0 368.6 jit_solution(13098753393832968978)
XLA Ops:
  8.6 7.2 %all-to-all-start.1 = ((bf16[256,16,4]{0,2,1:T(4,128)(2,1)}), bf16[256,16,4]{0,2,1:T(4,128)(2,1)S(1)}, u32[]{:S(2)}, u32[]{:S(2)}) async-start(bf16[256,16,4]{0,2,1:T(4,128)(2,1)} %reshape.131), calls=%async_computation.1 | async-start | bytes 65536 | tf_op jit(solution)/shard_map/all_to_all | solution.py:116
  15.7 3.3 copy.76
  19.0 4.1 %copy.77 = bf16[256,4096]{0,1:T(8,128)(2,1)} copy(bf16[256,4096]{1,0:T(8,128)(2,1)} %param.13) | data formatting | bytes 4194304 | tf_op args[6]
  23.1 3.9 %pad_maximum_fusion = bf16[256,16,512]{0,2,1:T(8,128)(2,1)} fusion(bf16[256,16,256]{0,2,1:T(8,128)(2,1)} %bitcast.190, bf16[256,16,256]{0,2,1:T(8,128)(2,1)S(1)} %bitcast.189), kind=kLoop, calls=%fused_computation.19 | loop fusion | flops 8388608 | bytes 8388608 | tf_op jit(solution)/shard_map/concatenate | solution.py:112
  27.0 7.1 %all-to-all-start = ((bf16[256,16,512]{0,2,1:T(8,128)(2,1)}), bf16[256,16,512]{0,2,1:T(8,128)(2,1)}, u32[]{:S(2)}, u32[]{:S(2)}) async-start(bf16[256,16,512]{0,2,1:T(8,128)(2,1)} %pad_maximum_fusion), calls=%async_computation | async-start | bytes 8388608 | tf_op jit(solution)/shard_map/all_to_all | solution.py:115
  36.9 104.5 %all-gather.2.cloned.1.call-done = bf16[4096,256]{1,0:T(8,128)(2,1)} async-done(((bf16[256,256]{1,0:T(8,128)(2,1)}), bf16[4096,256]{1,0:T(8,128)(2,1)}) %all-gather.2.cloned.1.call-update) | async-done | bytes 2097168 | tf_op jit(solution)/shard_map/all_gather | solution.py:96
  147.4 6.5 %copy.78 = bf16[16,256,1,512]{3,1,0,2:T(8,128)(2,1)} copy(bf16[16,256,1,512]{1,3,0,2:T(8,128)(2,1)} %bitcast.3) | data formatting | bytes 8388608 | tf_op jit(solution)/shard_map/all_to_all | solution.py:115
  153.9 4.5 %fusion.114 = (bf16[4096,256]{1,0:T(8,128)(2,1)}, bf16[4096,256]{1,0:T(8,128)(2,1)}) fusion(bf16[4096,512]{1,0:T(8,128)(2,1)} %bitcast.180), kind=kLoop, calls=%fused_computation.130 | loop fusion | bytes 8388608 | tf_op jit(solution)/shard_map/slice | solution.py:120
  161.3 4.3 %copy.79 = bf16[4096,256]{0,1:T(8,128)(2,1)} copy(bf16[4096,256]{1,0:T(8,128)(2,1)} %get-tuple-element.26) | data formatting | bytes 4194304 | tf_op jit(solution)/shard_map/slice | solution.py:120
  165.6 8.1 %multiply_reduce_fusion.4 = (f32[4,16]{1,0:T(4,128)}, f32[4,16,64,128]{3,2,1,0:T(8,128)S(1)}) fusion(f32[16,256,128]{1,2,0:T(8,128)} %copy.81, f32[4,16,256]{2,1,0:T(8,128)S(1)} %get-tuple-element.36, bf16[4,8,16,8,256]{4,3,2,1,0:T(8,128)(2,1)} %bitcast.175), kind=kOutput, calls=%fused_computation.41 | convolution fusion | flops 1613758464 | bytes 6357248 | tf_op jit(solution)/shard_map/transpose(jvp(vmap(kin,kpn->kip)))/dot_general | solution.py:51
  176.9 4.5 %fusion.10 = (f32[4,16,256]{2,0,1:T(4,128)S(1)}, f32[16,4,64,256]{3,2,1,0:T(8,128)}) fusion(bf16[4,8,16,8,256]{4,3,2,1,0:T(8,128)(2,1)S(1)} %bitcast.167, bf16[16,256,128,1]{2,1,3,0:T(8,128)(2,1)S(1)} %bitcast.172, f32[16,4,64,128]{3,0,2,1:T(8,128)S(1)} %fusion.44), kind=kOutput, calls=%fused_computation.18 | convolution fusion | flops 1613742080 | bytes 9502720 | tf_op jit(solution)/shard_map/transpose(jvp(vmap(kjp,kjn->kpn)))/dot_general | solution.py:38
  181.4 15.2 %fusion.5 = (f32[4,16,256]{2,1,0:T(8,128)}, f32[4,16,256]{2,1,0:T(8,128)}, f32[4,16,256]{2,1,0:T(8,128)S(1)}, f32[16,256,256]{2,1,0:T(8,128)S(1)}, f32[4,16,256,256]{3,2,1,0:T(8,128)}) fusion(f32[4,16,256]{2,1,0:T(8,128)S(1)} %bitcast.200, f32[4,16,256]{2,1,0:T(8,128)S(1)} %get-tuple-element.37, f32[16,256,256]{2,1,0:T(8,128)S(1)} %copy-done.13, ...), kind=kOutput, calls=%fused_computation.9 | convolution fusion | flops 594493440 | bytes 29753344 | tf_op jit(solution)/shard_map/transpose(jvp(vmap(kij,kjp->kip)))/dot_general | solution.py:35
  197.5 4.9 %fusion.118 = f32[16,256,128]{2,1,0:T(8,128)} fusion(f32[16,256,256]{2,1,0:T(8,128)S(1)} %get-tuple-element.15, bf16[16,256,128]{2,1,0:T(8,128)(2,1)S(1)} %bitcast.184), kind=kOutput, calls=%fused_computation.134 | convolution fusion | flops 1610612736 | bytes 7340032 | tf_op jit(solution)/shard_map/transpose(jvp(vmap(kin,kjn->kij)))/dot_general | solution.py:31
  208.9 7.1 %multiply_reduce_fusion.2 = (f32[4,16,256]{2,1,0:T(8,128)}, f32[16,256,128]{1,2,0:T(8,128)}) fusion(f32[16,256,128]{1,2,0:T(8,128)S(1)} %copy-done.14, f32[4,16,256]{2,1,0:T(8,128)S(1)} %copy-done.18, f32[4,16,64,128]{3,1,2,0:T(8,128)S(1)} %fusion.47, bf16[4,8,16,8,256]{4,3,2,1,0:T(8,128)(2,1)S(1)} %bitcast.177), kind=kOutput, calls=%fused_computation.10 | convolution fusion | flops 1618460672 | bytes 8519680 | tf_op jit(solution)/shard_map/transpose(jvp(vmap(kin,kpn->kip)))/dot_general | solution.py:51
  218.9 5.2 %convolution_add_fusion = f32[16,256,128]{2,1,0:T(8,128)S(1)} fusion(f32[16,256,128]{2,1,0:T(8,128)} %copy.100, f32[16,256,256]{2,1,0:T(8,128)} %copy-done.6, bf16[16,256,128]{2,1,0:T(8,128)(2,1)S(1)} %bitcast.174), kind=kOutput, calls=%fused_computation.56 | convolution fusion | flops 1611137024 | bytes 9437184 | tf_op jit(solution)/shard_map/transpose(jvp(vmap(kin,kjn->kij)))/dot_general | solution.py:31
  224.2 9.1 %broadcast_select_fusion.1 = (f32[16,256,128]{2,1,0:T(8,128)}, f32[16,256,128]{2,1,0:T(8,128)}) fusion(f32[16,256,128]{2,1,0:T(8,128)S(1)} %convolution_add_fusion, pred[]{:T(512)S(6)} %eq.11, f32[16,256,128]{2,1,0:T(8,128)S(1)} %copy-done.10, f32[16,4,64,128]{3,0,2,1:T(8,128)S(1)} %copy-done.1, f32[4,16,256]{2,0,1:T(4,128)S(1)} %copy.80, ...), kind=kOutput, calls=%fused_computation.70 | convolution fusion | flops 1614282752 | bytes 12648449 | tf_op jit(solution)/shard_map/transpose(jvp(vmap(kjp,kjn->kpn)))/dot_general | solution.py:38
  233.6 5.3 %fusion.113 = (f32[4,16]{1,0:T(4,128)S(1)}, f32[4,16]{1,0:T(4,128)S(1)}) fusion(f32[4,16]{1,0:T(4,128)S(1)} %get-tuple-element.38, f32[4,16]{1,0:T(4,128)S(1)} %get-tuple-element.21, f32[16,4,64,128]{3,2,1,0:T(8,128)S(1)} %copy-done.3, f32[4,16,64,128]{3,2,1,0:T(8,128)S(1)} %copy-done.12, pred[16,16]{1,0:T(8,128)(4,1)S(1)} %iota_compare_fusion.6), kind=kOutput, calls=%fused_computation.129 | convolution fusion | flops 100669312 | bytes 4195584 | tf_op jit(solution)/shard_map/transpose(jvp(vmap(kj,jpn->kpn)))/dot_general | solution.py:47
  240.2 5.5 %all-to-all-start.4 = ((bf16[16,256,4]{1,2,0:T(4,128)(2,1)}), bf16[16,256,4]{1,2,0:T(4,128)(2,1)S(1)}, u32[]{:S(2)}, u32[]{:S(2)}) async-start(bf16[16,256,4]{1,2,0:T(4,128)(2,1)} %bitcast.41), calls=%async_computation.4 | async-start | bytes 65536 | tf_op jit(solution)/shard_map/all_to_all | solution.py:126
  245.7 3.1 bitcast_add_fusion.1
  250.9 6.6 %all-to-all-start.3 = ((f32[16,256,128]{2,1,0:T(8,128)}), f32[16,256,128]{2,1,0:T(8,128)}, u32[]{:S(2)}, u32[]{:S(2)}) async-start(f32[16,256,128]{2,1,0:T(8,128)} %bitcast.185), calls=%async_computation.3 | async-start | bytes 4194304 | tf_op jit(solution)/shard_map/all_to_all | solution.py:137
  257.6 10.8 %fusion.12 = f32[16,4,8,8,256]{4,3,2,1,0:T(8,128)S(1)} fusion(f32[16,4,64,256]{3,2,1,0:T(8,128)} %get-tuple-element.40, f32[4,16,256]{2,0,1:T(4,128)S(1)} %copy.80, bf16[4,8,16,8,256]{4,3,2,1,0:T(8,128)(2,1)S(1)} %bitcast.178, f32[4,16,256,256]{3,2,1,0:T(8,128)} %get-tuple-element.22), kind=kOutput, calls=%fused_computation.22 | convolution fusion | flops 3223322624 | bytes 27328512 | tf_op jit(solution)/shard_map/transpose(jvp(vmap(kij,kjp->kip)))/dot_general | solution.py:35
  272.4 33.2 %all-to-all-done.3 = f32[16,256,128]{2,1,0:T(8,128)} async-done(((f32[16,256,128]{2,1,0:T(8,128)}), f32[16,256,128]{2,1,0:T(8,128)}, u32[]{:S(2)}, u32[]{:S(2)}) %all-to-all-start.3) | async-done | bytes 2097184 | tf_op jit(solution)/shard_map/all_to_all | solution.py:137
  305.6 4.7 %all-to-all-start.2 = ((bf16[16,256,256]{1,2,0:T(8,128)(2,1)}), bf16[16,256,256]{1,2,0:T(8,128)(2,1)S(1)}, u32[]{:S(2)}, u32[]{:S(2)}) async-start(bf16[16,256,256]{1,2,0:T(8,128)(2,1)} %copy.90), calls=%async_computation.2 | async-start | bytes 4194304 | tf_op jit(solution)/shard_map/all_to_all | solution.py:123
  312.8 45.2 %all-to-all-done.2 = bf16[16,256,256]{1,2,0:T(8,128)(2,1)S(1)} async-done(((bf16[16,256,256]{1,2,0:T(8,128)(2,1)}), bf16[16,256,256]{1,2,0:T(8,128)(2,1)S(1)}, u32[]{:S(2)}, u32[]{:S(2)}) %all-to-all-start.2) | async-done | bytes 2097184 | tf_op jit(solution)/shard_map/all_to_all | solution.py:123
  (105 shorter events, 40.1 us)
Async XLA Ops:
  8.6 18.4 %all-to-all-start.1 = ((bf16[256,16,4]{0,2,1:T(4,128)(2,1)}), bf16[256,16,4]{0,2,1:T(4,128)(2,1)S(1)}, u32[]{:S(2)}, u32[]{:S(2)}) async-start(bf16[256,16,4]{0,2,1:T(4,128)(2,1)} %reshape.131), calls=%async_computation.1 | async-start | bytes 65536 | tf_op jit(solution)/shard_map/all_to_all | solution.py:116
  27.0 7.1 %copy-start.21 = (bf16[256,128]{1,0:T(8,128)(2,1)S(1)}, bf16[256,128]{1,0:T(8,128)(2,1)}, u32[]{:S(2)}) copy-start(bf16[256,128]{1,0:T(8,128)(2,1)} %param.9) | copy-start | bytes 196612
  27.0 7.1 %copy-start.22 = (bf16[256,128]{1,0:T(8,128)(2,1)S(1)}, bf16[256,128]{1,0:T(8,128)(2,1)}, u32[]{:S(2)}) copy-start(bf16[256,128]{1,0:T(8,128)(2,1)} %param.8) | copy-start | bytes 196612
  27.0 7.8 %copy-start.27 = (f32[64]{0:T(128)S(1)}, f32[64]{0:T(128)}, u32[]{:S(2)}) copy-start(f32[64]{0:T(128)} %param.11) | copy-start | bytes 772
  27.0 120.4 %all-to-all-start = ((bf16[256,16,512]{0,2,1:T(8,128)(2,1)}), bf16[256,16,512]{0,2,1:T(8,128)(2,1)}, u32[]{:S(2)}, u32[]{:S(2)}) async-start(bf16[256,16,512]{0,2,1:T(8,128)(2,1)} %pad_maximum_fusion), calls=%async_computation | async-start | bytes 8388608 | tf_op jit(solution)/shard_map/all_to_all | solution.py:115
  34.0 107.3 %all-gather.2.cloned.1.call-start = ((), (), s32[]{:S(2)}) async-start(), calls=%async_computation.5 | async-start | bytes 2228224 | tf_op jit(solution)/shard_map/all_gather | solution.py:96
  36.0 129.6 %copy-start.17 = (f32[4,16,256]{2,1,0:T(8,128)}, f32[4,16,256]{2,1,0:T(8,128)S(1)}, u32[]{:S(2)}) copy-start(f32[4,16,256]{2,1,0:T(8,128)S(1)} %get-tuple-element.36) | copy-start | bytes 196612
  181.4 16.1 %copy-start.8 = (bf16[4096,128]{1,0:T(8,128)(2,1)S(1)}, bf16[4096,128]{1,0:T(8,128)(2,1)}, u32[]{:S(2)}) copy-start(bf16[4096,128]{1,0:T(8,128)(2,1)} %copy-done.7) | copy-start | bytes 3145732
  196.6 5.8 %copy-start.6 = (f32[16,256,256]{2,1,0:T(8,128)}, f32[16,256,256]{2,1,0:T(8,128)S(1)}, u32[]{:S(2)}) copy-start(f32[16,256,256]{2,1,0:T(8,128)S(1)} %get-tuple-element.15) | copy-start | bytes 12582916
  224.2 9.2 %copy-start.3 = (f32[16,4,64,128]{3,2,1,0:T(8,128)S(1)}, f32[16,4,64,128]{3,2,1,0:T(8,128)}, u32[]{:S(2)}) copy-start(f32[16,4,64,128]{3,2,1,0:T(8,128)} %copy-done.2) | copy-start | bytes 6291460
  224.2 9.2 %copy-start.12 = (f32[4,16,64,128]{3,2,1,0:T(8,128)S(1)}, f32[4,16,64,128]{3,2,1,0:T(8,128)}, u32[]{:S(2)}) copy-start(f32[4,16,64,128]{3,2,1,0:T(8,128)} %copy-done.11) | copy-start | bytes 6291460
  233.3 12.4 %collective-permute-start = (f32[4096,128]{1,0:T(8,128)}, f32[4096,128]{1,0:T(8,128)}, u32[]{:S(2)}, u32[]{:S(2)}) collective-permute-start(f32[4096,128]{1,0:T(8,128)} %bitcast.35), channel_id=1, source_target_pairs={{0,1},{1,0},{2,3},{3,2},{4,5},{5,4},{6,7},{7,6},{8,9},{9,8},{10,11... | collective-permute-start | bytes 6291464 | tf_op jit(solution)/shard_map/ppermute | solution.py:136
  233.5 5.3 %copy-start.24 = (f32[4,16]{1,0:T(4,128)S(1)}, f32[4,16]{1,0:T(4,128)}, u32[]{:S(2)}) copy-start(f32[4,16]{1,0:T(4,128)} %get-tuple-element.31) | copy-start | bytes 772
  233.5 5.6 %copy-start.15 = (f32[4,16,256]{2,1,0:T(8,128)S(1)}, f32[4,16,256]{2,1,0:T(8,128)}, u32[]{:S(2)}) copy-start(f32[4,16,256]{2,1,0:T(8,128)} %get-tuple-element.12) | copy-start | bytes 196612
  233.5 5.6 %copy-start.16 = (f32[4,16,256]{2,1,0:T(8,128)S(1)}, f32[4,16,256]{2,1,0:T(8,128)}, u32[]{:S(2)}) copy-start(f32[4,16,256]{2,1,0:T(8,128)} %get-tuple-element.13) | copy-start | bytes 196612
  233.5 5.6 %copy-start.19 = (f32[4,16,256]{2,1,0:T(8,128)S(1)}, f32[4,16,256]{2,1,0:T(8,128)}, u32[]{:S(2)}) copy-start(f32[4,16,256]{2,1,0:T(8,128)} %get-tuple-element.16) | copy-start | bytes 196612
  233.5 5.9 %copy-start.26 = (f32[4]{0:T(128)S(1)}, f32[4]{0:T(128)}, u32[]{:S(2)}) copy-start(f32[4]{0:T(128)} %copy-done.25) | copy-start | bytes 52
  233.5 12.2 %copy-start.9 = (f32[16,256,128]{2,1,0:T(8,128)S(1)}, f32[16,256,128]{2,1,0:T(8,128)}, u32[]{:S(2)}) copy-start(f32[16,256,128]{2,1,0:T(8,128)} %get-tuple-element.23) | copy-start | bytes 6291460
  240.2 10.8 %all-to-all-start.4 = ((bf16[16,256,4]{1,2,0:T(4,128)(2,1)}), bf16[16,256,4]{1,2,0:T(4,128)(2,1)S(1)}, u32[]{:S(2)}, u32[]{:S(2)}) async-start(bf16[16,256,4]{1,2,0:T(4,128)(2,1)} %bitcast.41), calls=%async_computation.4 | async-start | bytes 65536 | tf_op jit(solution)/shard_map/all_to_all | solution.py:126
  250.9 6.6 %copy-start.28 = (f32[64]{0:T(128)S(1)}, f32[64]{0:T(128)}, u32[]{:S(2)}) copy-start(f32[64]{0:T(128)} %param.12) | copy-start | bytes 772
  250.9 6.7 %copy-start.5 = (bf16[4096,256]{0,1:T(8,128)(2,1)S(1)}, bf16[4096,256]{0,1:T(8,128)(2,1)}, u32[]{:S(2)}) copy-start(bf16[4096,256]{0,1:T(8,128)(2,1)} %copy.79) | copy-start | bytes 6291460
  250.9 54.6 %all-to-all-start.3 = ((f32[16,256,128]{2,1,0:T(8,128)}), f32[16,256,128]{2,1,0:T(8,128)}, u32[]{:S(2)}, u32[]{:S(2)}) async-start(f32[16,256,128]{2,1,0:T(8,128)} %bitcast.185), calls=%async_computation.3 | async-start | bytes 4194304 | tf_op jit(solution)/shard_map/all_to_all | solution.py:137
  305.6 52.4 %all-to-all-start.2 = ((bf16[16,256,256]{1,2,0:T(8,128)(2,1)}), bf16[16,256,256]{1,2,0:T(8,128)(2,1)S(1)}, u32[]{:S(2)}, u32[]{:S(2)}) async-start(bf16[16,256,256]{1,2,0:T(8,128)(2,1)} %copy.90), calls=%async_computation.2 | async-start | bytes 4194304 | tf_op jit(solution)/shard_map/all_to_all | solution.py:123
  312.0 48.8 %collective-permute-start.1 = (f32[256,128]{1,0:T(8,128)S(1)}, f32[256,128]{1,0:T(8,128)S(1)}, u32[]{:S(2)}, u32[]{:S(2)}) collective-permute-start(f32[256,128]{1,0:T(8,128)S(1)} %reduce_sum.107), channel_id=1, source_target_pairs={{0,1},{1,0},{2,3},{3,2},{4,5},{5,4},{6,7},{7,6},{8,9},{9,8},{10,11... | collective-permute-start | bytes 393224 | tf_op jit(solution)/shard_map/ppermute | solution.py:139
  (14 other events, 52.8 us)
Sparse Core Ops, SparseCore 0:
  38.2 103.1 all-gather.1
